TPU v7x, 128 devices: a whole 4x4x4 slice. The times are simulated.
128 devices in a mesh: freq: 8 (over z_hi, x), blk: 16 (over y, z_lo, core).
Axes of the slice: x: 4, y: 4, z: 4 (z_hi: 2, z_lo: 2; z = z_hi * 2 + z_lo), core: 2. Of those that a mesh axis runs over, the one named last changes fastest.
Arguments:
- traces: bfloat16 [2048, 2048, 256], P('blk', 'freq'), may hold values from -6 to 6
- signature: float32 [8, 2], P('freq'), may hold values from 0.5 to 1.5
Outputs:
- multiples: float32 [8, 2, 2048, 2048], P('freq', None, 'blk')
All inputs are finite; a program needn't handle non-finite values.
Results may differ from a plain program's by a relative error of at most 0.0035.
Values sent between devices are 32-bit elements; how exact they have to be, the bound alone decides.
No kernel may reach another device: no remote copies, remote signals or barrier semaphores. Data moves between devices by JAX's collectives and lax.ppermute only.
A program may use at most 256 MiB of HBM per device.

v0:
```python
import math
import jax
import jax.numpy as jnp
from jax import lax
from jax.sharding import PartitionSpec as P

BIN0 = 4
BINSTEP = 3
GROUP = 4


def make_table(freqs, samples):
    bins = BIN0 + BINSTEP * jnp.arange(freqs, dtype=jnp.int32)
    steps = jnp.arange(samples, dtype=jnp.int32)
    phase = steps[:, None] * bins[None, :] % samples
    angle = phase.astype(jnp.float32) * (2.0 * math.pi / samples)
    scale = 1.0 / math.sqrt(samples)
    table = jnp.concatenate([jnp.cos(angle) * scale, -jnp.sin(angle) * scale], axis=1)
    return table.astype(jnp.bfloat16)


def xor_perm(n, m):
    return [(i, i ^ m) for i in range(n)]


def shift_perm(n, s):
    return [(i, (i + s) % n) for i in range(n)]


def on_device(traces, signature):
    src_rows, rec_cols, samples = traces.shape
    freqs = lax.axis_size("freq")
    nblk = lax.axis_size("blk")
    ny = nblk // GROUP
    assert ny == 4 and nblk % GROUP == 0
    table = make_table(freqs, samples)
    projected = jnp.einsum("srt,tc->csr", traces, table, preferred_element_type=jnp.float32)
    projected = projected.reshape(2, freqs, src_rows, rec_cols)
    spectra = lax.all_to_all(projected, "freq", split_axis=1, concat_axis=3, tiled=True)
    own = spectra[:, 0]
    n = own.shape[2]
    rb = src_rows
    gw = GROUP * rb
    cw = n // GROUP
    b = lax.axis_index("blk")
    p = b % GROUP
    y = b // GROUP
    q1 = lax.ppermute(own, "blk", xor_perm(nblk, 1))
    q2 = lax.ppermute(own, "blk", xor_perm(nblk, 2))
    q3 = lax.ppermute(q2, "blk", xor_perm(nblk, 1))
    rows = jnp.concatenate([own, q1, q2, q3], axis=1)
    piece = lax.dynamic_slice_in_dim(rows, p * cw, cw, axis=2)
    l5 = rows.reshape(2, gw, ny, GROUP, rb)
    lx = jnp.concatenate(
        [lax.dynamic_slice_in_dim(l5, p ^ m, 1, axis=3) for m in range(GROUP)], axis=3
    ).reshape(2, gw, n)

    def contrib(g, pc, lo, hi):
        lg = lax.dynamic_slice_in_dim(lx, g * gw + lo * rb, (hi - lo) * rb, axis=2)
        return jnp.einsum(
            "aik,bkj->abij",
            lg,
            pc,
            precision=lax.Precision.HIGH,
            preferred_element_type=jnp.float32,
        )

    up = shift_perm(nblk, GROUP)
    dn = shift_perm(nblk, -GROUP)
    r_up = lax.ppermute(piece, "blk", up)
    r_dn = lax.ppermute(piece, "blk", dn)
    half = gw // 2
    f_up = lax.ppermute(r_up[:, :half], "blk", up)
    f_dn = lax.ppermute(r_dn[:, half:], "blk", dn)
    t = contrib(y, piece, 0, GROUP)
    t = t + contrib((y - 1) % ny, r_up, 0, GROUP)
    t = t + contrib((y + 1) % ny, r_dn, 0, GROUP)
    t = t + contrib((y + 2) % ny, f_up, 0, GROUP // 2)
    t = t + contrib((y + 2) % ny, f_dn, GROUP // 2, GROUP)
    prod_re = t[0, 0] - t[1, 1]
    prod_im = t[0, 1] + t[1, 0]
    scale = 1.0 / math.sqrt(n)
    w_re = signature[0, 0]
    w_im = signature[0, 1]
    out_re = -(w_re * prod_re - w_im * prod_im) * scale
    out_im = -(w_re * prod_im + w_im * prod_re) * scale
    blk_out = jnp.stack([out_re, out_im], axis=0)
    parts = [blk_out[:, :rb]]
    for m in range(1, GROUP):
        parts.append(lax.ppermute(blk_out[:, m * rb : (m + 1) * rb], "blk", xor_perm(nblk, m)))
    stacked = jnp.stack(parts, axis=0)
    ordered = [lax.dynamic_index_in_dim(stacked, p ^ i, 0, keepdims=False) for i in range(GROUP)]
    out = jnp.concatenate(ordered, axis=2)
    return out[None]


def solution(mesh):
    return jax.shard_map(
        on_device,
        mesh=mesh,
        in_specs=(P("blk", "freq", None), P("freq", None)),
        out_specs=P("freq", None, "blk", None),
        check_vma=False,
    )
```

profile of v0, /device:TPU:1, one launch (start us, length us, event | category | flops | bytes accessed | tf_op | source)
XLA Modules:
  0.0 226.6 jit_solution(9673138914343612404)
XLA Ops:
  0.1 10.2 %convolution_bitcast_fusion = f32[2,8,128,256]{3,1,0,2:T(8,128)S(1)} fusion(bf16[128,256,256]{2,1,0:T(8,128)(2,1)} %param.2, bf16[256,8]{0,1:T(8,128)(2,1)S(1)} %get-tuple-element.18, bf16[256,8]{0,1:T(8,128)(2,1)S(1)} %get-tuple-element.17), kind=kOutput, calls=%fused_computation.29 | convolution fusion | flops 268451840 | bytes 18882560 | tf_op jit(solution)/shard_map/srt,tc->csr/dot_general | solution.py:37
  10.4 1.1 copy.44
  11.5 35.7 %all_to_all.15 = f32[2,8,128,256]{3,0,2,1:T(2,128)} all-to-all(f32[2,8,128,256]{3,0,2,1:T(2,128)S(1)} %copy.44), channel_id=1, replica_groups=mesh['freq'=8,'blk'=16] {'freq'}, dimensions={1} | all-to-all | bytes 4194304 | tf_op jit(solution)/shard_map/all_to_all | solution.py:39
  47.2 2.7 %copy.45 = f32[2,8,128,256]{2,3,1,0:T(8,128)S(1)} copy(f32[2,8,128,256]{3,0,2,1:T(2,128)} %all_to_all.15) | data formatting | bytes 4194304 | tf_op jit(solution)/shard_map/all_to_all | solution.py:39
  49.9 0.8 collective-permute-start.1
  50.7 2.0 collective-permute-start
  52.8 42.8 %collective-permute-done.1 = f32[2,128,2048]{1,2,0:T(8,128)} collective-permute-done((f32[2,128,2048]{1,2,0:T(8,128)S(1)}, f32[2,128,2048]{1,2,0:T(8,128)}, u32[]{:S(2)}, u32[]{:S(2)}) %collective-permute-start.1) | collective-permute-done | bytes 2097184 | tf_op jit(solution)/shard_map/ppermute | solution.py:49
  95.5 2.6 %collective-permute-start.2 = (f32[2,128,2048]{1,2,0:T(8,128)}, f32[2,128,2048]{1,2,0:T(8,128)}, u32[]{:S(2)}, u32[]{:S(2)}) collective-permute-start(f32[2,128,2048]{1,2,0:T(8,128)} %collective-permute-done.1), channel_id=1, source_target_pairs={{0,1},{1,0},{2,3},{3,2},{4,5},{5,4},{6,7},{7,6},{8,9},{9,8},{10,11... | collective-permute-start | bytes 6291464 | tf_op jit(solution)/shard_map/ppermute | solution.py:50
  98.1 4.1 %collective-permute-done.2 = f32[2,128,2048]{1,2,0:T(8,128)} collective-permute-done((f32[2,128,2048]{1,2,0:T(8,128)}, f32[2,128,2048]{1,2,0:T(8,128)}, u32[]{:S(2)}, u32[]{:S(2)}) %collective-permute-start.2) | collective-permute-done | bytes 2097184 | tf_op jit(solution)/shard_map/ppermute | solution.py:50
  102.3 2.8 %fusion.2 = f32[2,512,512]{1,2,0:T(8,128)} fusion(s32[]{:T(128)S(6)} %select_n.70, f32[2,128,2048]{1,2,0:T(8,128)S(1)} %bitcast.124, f32[2,128,2048]{1,2,0:T(8,128)} %collective-permute-done, f32[2,128,2048]{1,2,0:T(8,128)} %collective-permute-done.1, f32[2,128,2048]{1,2,0:T(8,128)} %collective-permute-done.2), kind=kLoop, calls=%fused_computation.15 | loop fusion | flops 1572864 | bytes 10485764 | tf_op jit(solution)/shard_map/concatenate | solution.py:51
  105.1 1.3 collective-permute-start.3
  106.4 1.4 collective-permute-start.4
  108.4 3.1 %pad_maximum_fusion = f32[2,512,4,4,128]{1,4,3,2,0:T(8,128)S(1)} fusion(f32[2,128,4,4,128]{1,4,3,2,0:T(8,128)} %bitcast.13, f32[2,128,4,4,128]{1,4,3,2,0:T(8,128)} %bitcast.12, f32[2,128,4,4,128]{1,4,3,2,0:T(8,128)} %bitcast.11, f32[2,128,4,4,128]{1,4,3,2,0:T(8,128)S(1)} %bitcast.125), kind=kLoop, calls=%fused_computation.4 | loop fusion | flops 6291456 | bytes 16777216 | tf_op jit(solution)/shard_map/concatenate | solution.py:51
  111.6 1.6 constant_dynamic-slice_fusion.7
  113.2 40.4 %collective-permute-done.3 = f32[2,512,512]{1,2,0:T(8,128)} collective-permute-done((f32[2,512,512]{1,2,0:T(8,128)}, f32[2,512,512]{1,2,0:T(8,128)}, u32[]{:S(2)}, u32[]{:S(2)}) %collective-permute-start.3) | collective-permute-done | bytes 2097184 | tf_op jit(solution)/shard_map/ppermute | solution.py:70
  153.5 1.3 slice.48
  154.9 1.2 pad_maximum_fusion.1
  156.2 1.3 slice.49
  157.5 2.9 %collective-permute-start.6 = (f32[2,256,512]{1,2,0:T(8,128)S(1)}, f32[2,256,512]{1,2,0:T(8,128)S(1)}, u32[]{:S(2)}, u32[]{:S(2)}) collective-permute-start(f32[2,256,512]{1,2,0:T(8,128)S(1)} %slice.49), channel_id=1, source_target_pairs={{0,12},{1,13},{2,14},{3,15},{4,0},{5,1},{6,2},{7,3},{8,4},{9,5},{1... | collective-permute-start | bytes 3145736 | tf_op jit(solution)/shard_map/ppermute | solution.py:74
  160.4 5.1 %fusion.5 = f32[2,512,2,512]{3,1,2,0:T(8,128)S(1)} fusion(f32[2,512,512]{1,2,0:T(8,128)} %collective-permute-done.3, f32[2,512,2048]{1,2,0:T(8,128)S(1)} %bitcast.117, s32[]{:T(128)S(6)} %select_n.78), kind=kOutput, calls=%fused_computation.20 | convolution fusion | flops 3221225472 | bytes 8388612 | tf_op jit(solution)/shard_map/aik,bkj->abij/dot_general | solution.py:60
  165.5 5.1 %fusion.3 = f32[2,512,2,512]{3,1,2,0:T(8,128)S(1)} fusion(f32[2,512,512]{1,2,0:T(8,128)} %collective-permute-done.4, f32[2,512,2048]{1,2,0:T(8,128)S(1)} %bitcast.118, s32[]{:T(128)S(6)} %select_n.80), kind=kOutput, calls=%fused_computation.18 | convolution fusion | flops 3221225472 | bytes 8388612 | tf_op jit(solution)/shard_map/aik,bkj->abij/dot_general | solution.py:60
  170.5 9.1 %collective-permute-done.5 = f32[2,256,512]{1,2,0:T(8,128)S(1)} collective-permute-done((f32[2,256,512]{1,2,0:T(8,128)S(1)}, f32[2,256,512]{1,2,0:T(8,128)S(1)}, u32[]{:S(2)}, u32[]{:S(2)}) %collective-permute-start.5) | collective-permute-done | bytes 1048608 | tf_op jit(solution)/shard_map/ppermute | solution.py:73
  179.7 1.8 fusion.17
  181.5 3.8 %fusion.15 = f32[2,512,2,512]{3,1,2,0:T(8,128)} fusion(f32[2,256,512]{1,2,0:T(8,128)S(1)} %collective-permute-done.6, f32[2,512,2048]{1,2,0:T(8,128)S(1)} %bitcast.120, s32[]{:T(128)S(6)} %select_n.83), kind=kOutput, calls=%fused_computation.34 | convolution fusion | flops 1610612736 | bytes 6291460 | tf_op jit(solution)/shard_map/aik,bkj->abij/dot_general | solution.py:60
  185.3 7.7 %add_bitcast_fusion = f32[2,2,512,512]{2,3,0,1:T(8,128)S(1)} fusion(f32[2,512,2,512]{3,1,2,0:T(8,128)} %fusion.15, f32[2,512,2,512]{3,1,2,0:T(8,128)S(1)} %fusion.17, f32[2,512,2,512]{3,1,2,0:T(8,128)S(1)} %fusion.3, f32[2,512,2,512]{3,1,2,0:T(8,128)S(1)} %fusion.5, f32[2,512,512]{1,2,0:T(8,128)} %fusion.2, f32[2,512,2048]{1,2,0:T(8,128)S(1)} %bitcast.121, ...), kind=kOutput, calls=%fused_computation.6 | convolution fusion | flops 3225419776 | bytes 25165828 | tf_op jit(solution)/shard_map/aik,bkj->abij/dot_general | solution.py:60
  193.0 1.8 fusion.23
  194.8 1.8 fusion.27
  196.8 2.3 %collective-permute-start.7 = (f32[2,128,512]{1,2,0:T(8,128)S(1)}, f32[2,128,512]{1,2,0:T(8,128)S(1)}, u32[]{:S(2)}, u32[]{:S(2)}) collective-permute-start(f32[2,128,512]{1,2,0:T(8,128)S(1)} %get-tuple-element.14), channel_id=1, source_target_pairs={{0,1},{1,0},{2,3},{3,2},{4,5},{5,4},{6,7},{7,6},{8,9},{9,8},{10,11... | collective-permute-start | bytes 1572872 | tf_op jit(solution)/shard_map/ppermute | solution.py:90
  199.8 1.0 collective-permute-start.9
  200.8 11.7 %collective-permute-done.8 = f32[2,128,512]{1,2,0:T(8,128)S(1)} collective-permute-done((f32[2,128,512]{1,2,0:T(8,128)S(1)}, f32[2,128,512]{1,2,0:T(8,128)S(1)}, u32[]{:S(2)}, u32[]{:S(2)}) %collective-permute-start.8) | collective-permute-done | bytes 524320 | tf_op jit(solution)/shard_map/ppermute | solution.py:90
  212.5 11.5 %collective-permute-done.9 = f32[2,128,512]{1,2,0:T(8,128)S(1)} collective-permute-done((f32[2,128,512]{1,2,0:T(8,128)S(1)}, f32[2,128,512]{1,2,0:T(8,128)S(1)}, u32[]{:S(2)}, u32[]{:S(2)}) %collective-permute-start.9) | collective-permute-done | bytes 524320 | tf_op jit(solution)/shard_map/ppermute | solution.py:90
  225.1 1.5 maximum_bitcast_fusion
  (18 shorter events, 2.9 us)
Async XLA Ops:
  49.9 45.6 %collective-permute-start.1 = (f32[2,128,2048]{1,2,0:T(8,128)S(1)}, f32[2,128,2048]{1,2,0:T(8,128)}, u32[]{:S(2)}, u32[]{:S(2)}) collective-permute-start(f32[2,128,2048]{1,2,0:T(8,128)S(1)} %bitcast.122), channel_id=1, source_target_pairs={{0,2},{1,3},{2,0},{3,1},{4,6},{5,7},{6,4},{7,5},{8,10},{9,11},{10,... | collective-permute-start | bytes 6291464 | tf_op jit(solution)/shard_map/ppermute | solution.py:49
  50.7 47.4 %collective-permute-start = (f32[2,128,2048]{1,2,0:T(8,128)S(1)}, f32[2,128,2048]{1,2,0:T(8,128)}, u32[]{:S(2)}, u32[]{:S(2)}) collective-permute-start(f32[2,128,2048]{1,2,0:T(8,128)S(1)} %bitcast.123), channel_id=1, source_target_pairs={{0,1},{1,0},{2,3},{3,2},{4,5},{5,4},{6,7},{7,6},{8,9},{9,8},{10,11... | collective-permute-start | bytes 6291464 | tf_op jit(solution)/shard_map/ppermute | solution.py:48
  95.5 6.7 %collective-permute-start.2 = (f32[2,128,2048]{1,2,0:T(8,128)}, f32[2,128,2048]{1,2,0:T(8,128)}, u32[]{:S(2)}, u32[]{:S(2)}) collective-permute-start(f32[2,128,2048]{1,2,0:T(8,128)} %collective-permute-done.1), channel_id=1, source_target_pairs={{0,1},{1,0},{2,3},{3,2},{4,5},{5,4},{6,7},{7,6},{8,9},{9,8},{10,11... | collective-permute-start | bytes 6291464 | tf_op jit(solution)/shard_map/ppermute | solution.py:50
  98.1 9.7 %copy-start = (f32[1,2]{1,0:T(1,128)S(1)}, f32[1,2]{1,0:T(1,128)}, u32[]{:S(2)}) copy-start(f32[1,2]{1,0:T(1,128)} %param.3) | copy-start | bytes 28
  105.1 48.5 %collective-permute-start.3 = (f32[2,512,512]{1,2,0:T(8,128)}, f32[2,512,512]{1,2,0:T(8,128)}, u32[]{:S(2)}, u32[]{:S(2)}) collective-permute-start(f32[2,512,512]{1,2,0:T(8,128)} %fusion.2), channel_id=1, source_target_pairs={{0,4},{1,5},{2,6},{3,7},{4,8},{5,9},{6,10},{7,11},{8,12},{9,13},{1... | collective-permute-start | bytes 6291464 | tf_op jit(solution)/shard_map/ppermute | solution.py:70
  106.4 49.8 %collective-permute-start.4 = (f32[2,512,512]{1,2,0:T(8,128)}, f32[2,512,512]{1,2,0:T(8,128)}, u32[]{:S(2)}, u32[]{:S(2)}) collective-permute-start(f32[2,512,512]{1,2,0:T(8,128)} %fusion.2), channel_id=1, source_target_pairs={{0,12},{1,13},{2,14},{3,15},{4,0},{5,1},{6,2},{7,3},{8,4},{9,5},{1... | collective-permute-start | bytes 6291464 | tf_op jit(solution)/shard_map/ppermute | solution.py:71
  154.8 24.8 %collective-permute-start.5 = (f32[2,256,512]{1,2,0:T(8,128)S(1)}, f32[2,256,512]{1,2,0:T(8,128)S(1)}, u32[]{:S(2)}, u32[]{:S(2)}) collective-permute-start(f32[2,256,512]{1,2,0:T(8,128)S(1)} %slice.48), channel_id=1, source_target_pairs={{0,4},{1,5},{2,6},{3,7},{4,8},{5,9},{6,10},{7,11},{8,12},{9,13},{1... | collective-permute-start | bytes 3145736 | tf_op jit(solution)/shard_map/ppermute | solution.py:73
  157.5 24.0 %collective-permute-start.6 = (f32[2,256,512]{1,2,0:T(8,128)S(1)}, f32[2,256,512]{1,2,0:T(8,128)S(1)}, u32[]{:S(2)}, u32[]{:S(2)}) collective-permute-start(f32[2,256,512]{1,2,0:T(8,128)S(1)} %slice.49), channel_id=1, source_target_pairs={{0,12},{1,13},{2,14},{3,15},{4,0},{5,1},{6,2},{7,3},{8,4},{9,5},{1... | collective-permute-start | bytes 3145736 | tf_op jit(solution)/shard_map/ppermute | solution.py:74
  196.8 4.0 %collective-permute-start.7 = (f32[2,128,512]{1,2,0:T(8,128)S(1)}, f32[2,128,512]{1,2,0:T(8,128)S(1)}, u32[]{:S(2)}, u32[]{:S(2)}) collective-permute-start(f32[2,128,512]{1,2,0:T(8,128)S(1)} %get-tuple-element.14), channel_id=1, source_target_pairs={{0,1},{1,0},{2,3},{3,2},{4,5},{5,4},{6,7},{7,6},{8,9},{9,8},{10,11... | collective-permute-start | bytes 1572872 | tf_op jit(solution)/shard_map/ppermute | solution.py:90
  199.1 13.4 %collective-permute-start.8 = (f32[2,128,512]{1,2,0:T(8,128)S(1)}, f32[2,128,512]{1,2,0:T(8,128)S(1)}, u32[]{:S(2)}, u32[]{:S(2)}) collective-permute-start(f32[2,128,512]{1,2,0:T(8,128)S(1)} %get-tuple-element.16), channel_id=1, source_target_pairs={{0,2},{1,3},{2,0},{3,1},{4,6},{5,7},{6,4},{7,5},{8,10},{9,11},{10,... | collective-permute-start | bytes 1572872 | tf_op jit(solution)/shard_map/ppermute | solution.py:90
  199.8 24.1 %collective-permute-start.9 = (f32[2,128,512]{1,2,0:T(8,128)S(1)}, f32[2,128,512]{1,2,0:T(8,128)S(1)}, u32[]{:S(2)}, u32[]{:S(2)}) collective-permute-start(f32[2,128,512]{1,2,0:T(8,128)S(1)} %get-tuple-element.15), channel_id=1, source_target_pairs={{0,3},{1,2},{2,1},{3,0},{4,7},{5,6},{6,5},{7,4},{8,11},{9,10},{10,... | collective-permute-start | bytes 1572872 | tf_op jit(solution)/shard_map/ppermute | solution.py:90
where the time goes:
time: 227 us
  waiting for transfers between devices  120 us (53%)
  blocking collectives  35.7 us (16%)
  matrix products  33.6 us (15%)
  starting transfers between devices  15.2 us (7%)
  other arithmetic  12.8 us (6%)
  local copies, waits for them, and re-layouts  9.57 us (4%)
    ppermute x1, waiting for transfers between devices, on_device(): q2 = lax.ppermute(own, 'blk', xor_perm(nblk, 2))  42.8 us
    ppermute x1, waiting for transfers between devices, on_device(): r_up = lax.ppermute(piece, 'blk', up)  40.4 us
    all_to_all x1, blocking collectives, on_device(): lax.all_to_all(projected, 'freq', split_axis=1, concat_axis=3, tiled=True)  35.7 us
    dot_general x5, matrix products, contrib(): jnp.einsum('aik,bkj->abij', lg, pc, precision=lax.Precision.HIGH, preferr...  23.4 us
    ppermute x3, waiting for transfers between devices, on_device(): lax.ppermute(blk_out[:, m * rb:(m + 1) * rb], 'blk', xor_perm(nblk, m))  23.2 us
    dot_general x1, matrix products, on_device(): jnp.einsum('srt,tc->csr', traces, table, preferred_element_type=jnp.float32)  10.2 us
    ppermute x1, waiting for transfers between devices, on_device(): f_up = lax.ppermute(r_up[:, :half], 'blk', up)  9.13 us
    concatenate x2, other arithmetic, on_device(): rows = jnp.concatenate([own, q1, q2, q3], axis=1)  5.96 us
  transfers between devices with their start and end apart: 10, of which 6 were waited for; matrix products, arithmetic and copies ran while one was open for 9% of the time, Pallas kernels for 0%

commit v1 on v0

--- a/solution.py
+++ b/solution.py
@@ -36,7 +36,12 @@
     table = make_table(freqs, samples)
     projected = jnp.einsum("srt,tc->csr", traces, table, preferred_element_type=jnp.float32)
     projected = projected.reshape(2, freqs, src_rows, rec_cols)
-    spectra = lax.all_to_all(projected, "freq", split_axis=1, concat_axis=3, tiled=True)
+    spectra = jnp.concatenate(
+        lax.all_to_all(
+            jnp.stack(jnp.split(projected, lax.axis_size("freq"), axis=1)), "freq", 0, 0
+        ),
+        axis=3,
+    )
     own = spectra[:, 0]
     n = own.shape[2]
     rb = src_rows

time: 227 us -> 237 us (1.044)
  local copies, waits for them, and re-layouts: 9.57 us -> 19 us
    unnamed x2 -> x17, local copies, waits for them, and re-layouts: 0.01 us -> 10.9 us
    all_to_all x1, local copies, waits for them, and re-layouts: 2.73 us -> 0.14 us  [on_device(): lax.all_to_all(jnp.stack(jnp.split(projected, lax.axis_size('freq'), axis...]
where the time goes in v1:
time: 237 us; the launch traced here: 236 us
  waiting for transfers between devices  120 us (51%)
  blocking collectives  35.6 us (15%)
  matrix products  33.6 us (14%)
  local copies, waits for them, and re-layouts  19 us (8%)
  starting transfers between devices  15.2 us (6%)
  other arithmetic  12.8 us (5%)
    ppermute x1, waiting for transfers between devices, on_device(): q2 = lax.ppermute(own, 'blk', xor_perm(nblk, 2))  42.8 us
    ppermute x1, waiting for transfers between devices, on_device(): r_up = lax.ppermute(piece, 'blk', up)  40.3 us
    all_to_all x1, blocking collectives, on_device(): lax.all_to_all(jnp.stack(jnp.split(projected, lax.axis_size('freq'), axis...  35.6 us
    dot_general x5, matrix products, contrib(): jnp.einsum('aik,bkj->abij', lg, pc, precision=lax.Precision.HIGH, preferr...  23.4 us
    ppermute x3, waiting for transfers between devices, on_device(): lax.ppermute(blk_out[:, m * rb:(m + 1) * rb], 'blk', xor_perm(nblk, m))  23.2 us
    unnamed x17, local copies, waits for them, and re-layouts  10.9 us
    dot_general x1, matrix products, on_device(): jnp.einsum('srt,tc->csr', traces, table, preferred_element_type=jnp.float32)  10.2 us
    ppermute x1, waiting for transfers between devices, on_device(): f_up = lax.ppermute(r_up[:, :half], 'blk', up)  9.13 us
  transfers between devices with their start and end apart: 10, of which 6 were waited for; matrix products, arithmetic and copies ran while one was open for 9% of the time, Pallas kernels for 0%

profile of v1, /device:TPU:1, one launch (start us, length us, event | category | flops | bytes accessed | tf_op | source)
XLA Modules:
  0.0 236.0 jit_solution(2262338947830233752)
XLA Ops:
  0.1 10.2 %convolution_bitcast_fusion = f32[2,8,128,256]{3,1,0,2:T(8,128)S(1)} fusion(bf16[128,256,256]{2,1,0:T(8,128)(2,1)} %param.2, bf16[256,8]{0,1:T(8,128)(2,1)S(1)} %get-tuple-element.26, bf16[256,8]{0,1:T(8,128)(2,1)S(1)} %get-tuple-element.25), kind=kOutput, calls=%fused_computation.29 | convolution fusion | flops 268451840 | bytes 18882560 | tf_op jit(solution)/shard_map/srt,tc->csr/dot_general | solution.py:37
  10.4 2.2 fusion.48
  12.6 1.8 copy.65
  15.3 1.8 copy.66
  17.1 1.8 copy.67
  23.5 35.6 %all_to_all.5 = f32[8,2,1,128,256]{3,4,1,2,0:T(8,128)S(1)} all-to-all(f32[8,2,1,128,256]{3,4,1,2,0:T(8,128)S(1)} %bitcast_dynamic-update-slice_fusion), channel_id=1, replica_groups=mesh['freq'=8,'blk'=16] {'freq'}, dimensions={0} | all-to-all | bytes 4194304 | tf_op jit(solution)/shard_map/all_to_all | solution.py:40
  60.1 2.0 collective-permute-start
  62.1 42.8 %collective-permute-done.1 = f32[2,128,2048]{1,2,0:T(8,128)} collective-permute-done((f32[2,128,2048]{1,2,0:T(8,128)S(1)}, f32[2,128,2048]{1,2,0:T(8,128)}, u32[]{:S(2)}, u32[]{:S(2)}) %collective-permute-start.1) | collective-permute-done | bytes 2097184 | tf_op jit(solution)/shard_map/ppermute | solution.py:54
  104.9 2.6 %collective-permute-start.2 = (f32[2,128,2048]{1,2,0:T(8,128)}, f32[2,128,2048]{1,2,0:T(8,128)}, u32[]{:S(2)}, u32[]{:S(2)}) collective-permute-start(f32[2,128,2048]{1,2,0:T(8,128)} %collective-permute-done.1), channel_id=1, source_target_pairs={{0,1},{1,0},{2,3},{3,2},{4,5},{5,4},{6,7},{7,6},{8,9},{9,8},{10,11... | collective-permute-start | bytes 6291464 | tf_op jit(solution)/shard_map/ppermute | solution.py:55
  107.5 4.1 %collective-permute-done.2 = f32[2,128,2048]{1,2,0:T(8,128)} collective-permute-done((f32[2,128,2048]{1,2,0:T(8,128)}, f32[2,128,2048]{1,2,0:T(8,128)}, u32[]{:S(2)}, u32[]{:S(2)}) %collective-permute-start.2) | collective-permute-done | bytes 2097184 | tf_op jit(solution)/shard_map/ppermute | solution.py:55
  111.6 2.8 %fusion.2 = f32[2,512,512]{1,2,0:T(8,128)} fusion(s32[]{:T(128)S(6)} %select_n.70, f32[2,128,2048]{1,2,0:T(8,128)S(1)} %bitcast.138, f32[2,128,2048]{1,2,0:T(8,128)} %collective-permute-done, f32[2,128,2048]{1,2,0:T(8,128)} %collective-permute-done.1, f32[2,128,2048]{1,2,0:T(8,128)} %collective-permute-done.2), kind=kLoop, calls=%fused_computation.15 | loop fusion | flops 1572864 | bytes 10485764 | tf_op jit(solution)/shard_map/concatenate | solution.py:56
  114.5 1.3 collective-permute-start.3
  115.8 1.4 collective-permute-start.4
  117.8 3.1 %pad_maximum_fusion = f32[2,512,4,4,128]{1,4,3,2,0:T(8,128)S(1)} fusion(f32[2,128,4,4,128]{1,4,3,2,0:T(8,128)} %bitcast.19, f32[2,128,4,4,128]{1,4,3,2,0:T(8,128)} %bitcast.18, f32[2,128,4,4,128]{1,4,3,2,0:T(8,128)} %bitcast.17, f32[2,128,4,4,128]{1,4,3,2,0:T(8,128)S(1)} %bitcast.139), kind=kLoop, calls=%fused_computation.4 | loop fusion | flops 6291456 | bytes 16777216 | tf_op jit(solution)/shard_map/concatenate | solution.py:56
  121.0 1.6 constant_dynamic-slice_fusion.7
  122.6 40.3 %collective-permute-done.3 = f32[2,512,512]{1,2,0:T(8,128)} collective-permute-done((f32[2,512,512]{1,2,0:T(8,128)}, f32[2,512,512]{1,2,0:T(8,128)}, u32[]{:S(2)}, u32[]{:S(2)}) %collective-permute-start.3) | collective-permute-done | bytes 2097184 | tf_op jit(solution)/shard_map/ppermute | solution.py:75
  162.9 1.3 slice.48
  164.3 1.2 pad_maximum_fusion.1
  165.6 1.3 slice.49
  166.9 2.9 %collective-permute-start.6 = (f32[2,256,512]{1,2,0:T(8,128)S(1)}, f32[2,256,512]{1,2,0:T(8,128)S(1)}, u32[]{:S(2)}, u32[]{:S(2)}) collective-permute-start(f32[2,256,512]{1,2,0:T(8,128)S(1)} %slice.49), channel_id=1, source_target_pairs={{0,12},{1,13},{2,14},{3,15},{4,0},{5,1},{6,2},{7,3},{8,4},{9,5},{1... | collective-permute-start | bytes 3145736 | tf_op jit(solution)/shard_map/ppermute | solution.py:79
  169.7 5.1 %fusion.5 = f32[2,512,2,512]{3,1,2,0:T(8,128)S(1)} fusion(f32[2,512,512]{1,2,0:T(8,128)} %collective-permute-done.3, f32[2,512,2048]{1,2,0:T(8,128)S(1)} %bitcast.131, s32[]{:T(128)S(6)} %select_n.78), kind=kOutput, calls=%fused_computation.20 | convolution fusion | flops 3221225472 | bytes 8388612 | tf_op jit(solution)/shard_map/aik,bkj->abij/dot_general | solution.py:65
  174.8 5.1 %fusion.3 = f32[2,512,2,512]{3,1,2,0:T(8,128)S(1)} fusion(f32[2,512,512]{1,2,0:T(8,128)} %collective-permute-done.4, f32[2,512,2048]{1,2,0:T(8,128)S(1)} %bitcast.132, s32[]{:T(128)S(6)} %select_n.80), kind=kOutput, calls=%fused_computation.18 | convolution fusion | flops 3221225472 | bytes 8388612 | tf_op jit(solution)/shard_map/aik,bkj->abij/dot_general | solution.py:65
  179.9 9.1 %collective-permute-done.5 = f32[2,256,512]{1,2,0:T(8,128)S(1)} collective-permute-done((f32[2,256,512]{1,2,0:T(8,128)S(1)}, f32[2,256,512]{1,2,0:T(8,128)S(1)}, u32[]{:S(2)}, u32[]{:S(2)}) %collective-permute-start.5) | collective-permute-done | bytes 1048608 | tf_op jit(solution)/shard_map/ppermute | solution.py:78
  189.0 1.8 fusion.17
  190.9 3.8 %fusion.15 = f32[2,512,2,512]{3,1,2,0:T(8,128)} fusion(f32[2,256,512]{1,2,0:T(8,128)S(1)} %collective-permute-done.6, f32[2,512,2048]{1,2,0:T(8,128)S(1)} %bitcast.134, s32[]{:T(128)S(6)} %select_n.83), kind=kOutput, calls=%fused_computation.34 | convolution fusion | flops 1610612736 | bytes 6291460 | tf_op jit(solution)/shard_map/aik,bkj->abij/dot_general | solution.py:65
  194.7 7.7 %add_bitcast_fusion = f32[2,2,512,512]{2,3,0,1:T(8,128)S(1)} fusion(f32[2,512,2,512]{3,1,2,0:T(8,128)} %fusion.15, f32[2,512,2,512]{3,1,2,0:T(8,128)S(1)} %fusion.17, f32[2,512,2,512]{3,1,2,0:T(8,128)S(1)} %fusion.3, f32[2,512,2,512]{3,1,2,0:T(8,128)S(1)} %fusion.5, f32[2,512,512]{1,2,0:T(8,128)} %fusion.2, f32[2,512,2048]{1,2,0:T(8,128)S(1)} %bitcast.135, ...), kind=kOutput, calls=%fused_computation.6 | convolution fusion | flops 3225419776 | bytes 25165828 | tf_op jit(solution)/shard_map/aik,bkj->abij/dot_general | solution.py:65
  202.3 1.8 fusion.23
  204.2 1.8 fusion.27
  206.1 2.3 collective-permute-start.7
  210.2 11.7 %collective-permute-done.8 = f32[2,128,512]{1,2,0:T(8,128)S(1)} collective-permute-done((f32[2,128,512]{1,2,0:T(8,128)S(1)}, f32[2,128,512]{1,2,0:T(8,128)S(1)}, u32[]{:S(2)}, u32[]{:S(2)}) %collective-permute-start.8) | collective-permute-done | bytes 524320 | tf_op jit(solution)/shard_map/ppermute | solution.py:95
  221.8 11.5 %collective-permute-done.9 = f32[2,128,512]{1,2,0:T(8,128)S(1)} collective-permute-done((f32[2,128,512]{1,2,0:T(8,128)S(1)}, f32[2,128,512]{1,2,0:T(8,128)S(1)}, u32[]{:S(2)}, u32[]{:S(2)}) %collective-permute-start.9) | collective-permute-done | bytes 524320 | tf_op jit(solution)/shard_map/ppermute | solution.py:95
  234.5 1.5 maximum_bitcast_fusion
  (34 shorter events, 10.4 us)
Async XLA Ops:
  59.3 45.6 %collective-permute-start.1 = (f32[2,128,2048]{1,2,0:T(8,128)S(1)}, f32[2,128,2048]{1,2,0:T(8,128)}, u32[]{:S(2)}, u32[]{:S(2)}) collective-permute-start(f32[2,128,2048]{1,2,0:T(8,128)S(1)} %bitcast.136), channel_id=1, source_target_pairs={{0,2},{1,3},{2,0},{3,1},{4,6},{5,7},{6,4},{7,5},{8,10},{9,11},{10,... | collective-permute-start | bytes 6291464 | tf_op jit(solution)/shard_map/ppermute | solution.py:54
  60.1 47.4 %collective-permute-start = (f32[2,128,2048]{1,2,0:T(8,128)S(1)}, f32[2,128,2048]{1,2,0:T(8,128)}, u32[]{:S(2)}, u32[]{:S(2)}) collective-permute-start(f32[2,128,2048]{1,2,0:T(8,128)S(1)} %bitcast.137), channel_id=1, source_target_pairs={{0,1},{1,0},{2,3},{3,2},{4,5},{5,4},{6,7},{7,6},{8,9},{9,8},{10,11... | collective-permute-start | bytes 6291464 | tf_op jit(solution)/shard_map/ppermute | solution.py:53
  104.9 6.7 %collective-permute-start.2 = (f32[2,128,2048]{1,2,0:T(8,128)}, f32[2,128,2048]{1,2,0:T(8,128)}, u32[]{:S(2)}, u32[]{:S(2)}) collective-permute-start(f32[2,128,2048]{1,2,0:T(8,128)} %collective-permute-done.1), channel_id=1, source_target_pairs={{0,1},{1,0},{2,3},{3,2},{4,5},{5,4},{6,7},{7,6},{8,9},{9,8},{10,11... | collective-permute-start | bytes 6291464 | tf_op jit(solution)/shard_map/ppermute | solution.py:55
  107.5 9.7 %copy-start = (f32[1,2]{1,0:T(1,128)S(1)}, f32[1,2]{1,0:T(1,128)}, u32[]{:S(2)}) copy-start(f32[1,2]{1,0:T(1,128)} %param.3) | copy-start | bytes 28
  114.5 48.5 %collective-permute-start.3 = (f32[2,512,512]{1,2,0:T(8,128)}, f32[2,512,512]{1,2,0:T(8,128)}, u32[]{:S(2)}, u32[]{:S(2)}) collective-permute-start(f32[2,512,512]{1,2,0:T(8,128)} %fusion.2), channel_id=1, source_target_pairs={{0,4},{1,5},{2,6},{3,7},{4,8},{5,9},{6,10},{7,11},{8,12},{9,13},{1... | collective-permute-start | bytes 6291464 | tf_op jit(solution)/shard_map/ppermute | solution.py:75
  115.8 49.8 %collective-permute-start.4 = (f32[2,512,512]{1,2,0:T(8,128)}, f32[2,512,512]{1,2,0:T(8,128)}, u32[]{:S(2)}, u32[]{:S(2)}) collective-permute-start(f32[2,512,512]{1,2,0:T(8,128)} %fusion.2), channel_id=1, source_target_pairs={{0,12},{1,13},{2,14},{3,15},{4,0},{5,1},{6,2},{7,3},{8,4},{9,5},{1... | collective-permute-start | bytes 6291464 | tf_op jit(solution)/shard_map/ppermute | solution.py:76
  164.2 24.8 %collective-permute-start.5 = (f32[2,256,512]{1,2,0:T(8,128)S(1)}, f32[2,256,512]{1,2,0:T(8,128)S(1)}, u32[]{:S(2)}, u32[]{:S(2)}) collective-permute-start(f32[2,256,512]{1,2,0:T(8,128)S(1)} %slice.48), channel_id=1, source_target_pairs={{0,4},{1,5},{2,6},{3,7},{4,8},{5,9},{6,10},{7,11},{8,12},{9,13},{1... | collective-permute-start | bytes 3145736 | tf_op jit(solution)/shard_map/ppermute | solution.py:78
  166.9 24.0 %collective-permute-start.6 = (f32[2,256,512]{1,2,0:T(8,128)S(1)}, f32[2,256,512]{1,2,0:T(8,128)S(1)}, u32[]{:S(2)}, u32[]{:S(2)}) collective-permute-start(f32[2,256,512]{1,2,0:T(8,128)S(1)} %slice.49), channel_id=1, source_target_pairs={{0,12},{1,13},{2,14},{3,15},{4,0},{5,1},{6,2},{7,3},{8,4},{9,5},{1... | collective-permute-start | bytes 3145736 | tf_op jit(solution)/shard_map/ppermute | solution.py:79
  206.1 4.1 %collective-permute-start.7 = (f32[2,128,512]{1,2,0:T(8,128)S(1)}, f32[2,128,512]{1,2,0:T(8,128)S(1)}, u32[]{:S(2)}, u32[]{:S(2)}) collective-permute-start(f32[2,128,512]{1,2,0:T(8,128)S(1)} %get-tuple-element.14), channel_id=1, source_target_pairs={{0,1},{1,0},{2,3},{3,2},{4,5},{5,4},{6,7},{7,6},{8,9},{9,8},{10,11... | collective-permute-start | bytes 1572872 | tf_op jit(solution)/shard_map/ppermute | solution.py:95
  208.4 13.4 %collective-permute-start.8 = (f32[2,128,512]{1,2,0:T(8,128)S(1)}, f32[2,128,512]{1,2,0:T(8,128)S(1)}, u32[]{:S(2)}, u32[]{:S(2)}) collective-permute-start(f32[2,128,512]{1,2,0:T(8,128)S(1)} %get-tuple-element.16), channel_id=1, source_target_pairs={{0,2},{1,3},{2,0},{3,1},{4,6},{5,7},{6,4},{7,5},{8,10},{9,11},{10,... | collective-permute-start | bytes 1572872 | tf_op jit(solution)/shard_map/ppermute | solution.py:95
  209.2 24.1 %collective-permute-start.9 = (f32[2,128,512]{1,2,0:T(8,128)S(1)}, f32[2,128,512]{1,2,0:T(8,128)S(1)}, u32[]{:S(2)}, u32[]{:S(2)}) collective-permute-start(f32[2,128,512]{1,2,0:T(8,128)S(1)} %get-tuple-element.15), channel_id=1, source_target_pairs={{0,3},{1,2},{2,1},{3,0},{4,7},{5,6},{6,5},{7,4},{8,11},{9,10},{10,... | collective-permute-start | bytes 1572872 | tf_op jit(solution)/shard_map/ppermute | solution.py:95
